TPU v7x, 32 devices: a whole 2x2x4 slice. The times are simulated.
32 devices in a mesh: groups: 2 (over y), lat: 4 (over x, core), lon: 4 (over z).
Axes of the slice: x: 2, y: 2, z: 4, core: 2. Of those that a mesh axis runs over, the one named last changes fastest.
Arguments:
- fields: bfloat16 [512, 4, 512], P('groups', 'lat', 'lon'), parts along dimension 0, may hold values from -6 to 6
- upstream: bfloat16 [512, 4, 512], P('groups', 'lat', 'lon'), parts along dimension 0, may hold values from -6 to 6
- weights: bfloat16 [9, 256, 256], replicated, may hold values from -0.125 to 0.125
- filter_taps: bfloat16 [4, 9, 3, 2, 64], P('lat'), may hold values from -0.3125 to 0.3125
- cycle_counts: int32 [4], P('lat'), may hold values from 1 to 2, as said below
- cycle_blocks: int32 [4, 2], P('lat'), may hold values from -2 to 1, as said below
Outputs:
- outputs: bfloat16 [512, 4, 512], P('groups', 'lat', 'lon'), parts along dimension 0
- input_grad: bfloat16 [512, 4, 512], P('groups', 'lat', 'lon'), parts along dimension 0
- weight_grad: float32 [18, 256, 256], P('groups', 'lon'), parts along dimension 0
There are 2 independent parts, one for each index of `groups`. A program takes and returns all parts, laid end to end along the dimension named above; an argument that names none is the same for every part. Nothing has to cross between parts.
Inputs may be any that keep to these rules, and one draw needn't show every extreme that they name: Cycle i uses its first cycle_counts[i] slots; the first quarter of the cycles (at least one) uses all 2, the last cycle one. `cycle_blocks`: the 2 block numbers of a cycle are distinct; the first cycle holds the lowest and the highest.
All inputs are finite; a program needn't handle non-finite values.
Results may differ from a plain program's by a relative error of at most 0.0049.
Values may be sent and summed in bfloat16 or wider, within the bound.
No kernel may reach another device: no remote copies, remote signals or barrier semaphores. Data moves between devices by JAX's collectives and lax.ppermute only.
A program may use at most 64 MiB of HBM per device.

v0:
```python
import jax
import jax.numpy as jnp
from jax import lax
from jax.sharding import PartitionSpec as P

HALO = 128


def padded_2(cells, sides, width, closed):
    for axis, dim in sides:
        count = lax.axis_size(axis)
        ends = count if closed else count - 1
        head = lax.slice_in_dim(cells, 0, width, axis=dim)
        tail = lax.slice_in_dim(cells, cells.shape[dim] - width, cells.shape[dim], axis=dim)
        cells = jnp.concatenate(
            [
                lax.ppermute(tail, axis, [(i, (i + 1) % count) for i in range(ends)]),
                cells,
                lax.ppermute(head, axis, [((i + 1) % count, i) for i in range(ends)]),
            ],
            axis=dim,
        )
    return cells


def build_taps(filter_taps, cycle_counts, cycle_blocks):
    slot_total = cycle_blocks.shape[1]
    width_block = filter_taps.shape[4]
    offsets = jnp.arange(width_block, dtype=jnp.int32)
    places = HALO + width_block * cycle_blocks[:, :, None] + offsets[None, None, :]
    live_slots = jnp.arange(slot_total, dtype=jnp.int32)[None, :] < cycle_counts[:, None]
    positions = jnp.arange(2 * HALO, dtype=jnp.int32)
    onehot = jnp.where(
        (places[:, :, :, None] == positions) & live_slots[:, :, None, None], 1.0, 0.0
    ).astype(jnp.float32)
    return jnp.einsum("ikrst,istu->ikru", filter_taps.astype(jnp.float32), onehot)


def banded_matrix(tap_row, out_width, tap_reach):
    kernels = tap_row.shape[0]
    stencil_rows = tap_row.shape[1]
    window_len = out_width + tap_reach
    padded = jnp.concatenate(
        [tap_row, jnp.zeros((kernels, stencil_rows, window_len + 1 - tap_reach), tap_row.dtype)],
        axis=2,
    )
    repeated = jnp.tile(padded, (1, 1, out_width))[:, :, : out_width * window_len]
    repeated = repeated.reshape(kernels, stencil_rows, out_width, window_len)
    return jnp.transpose(repeated, (1, 3, 0, 2))


def body(fields, upstream, weights, filter_taps, cycle_counts, cycle_blocks):
    channels, lat_rows, lon_cols = fields.shape
    kernels = weights.shape[0]
    window_len = lon_cols + 2 * HALO
    tap_table = build_taps(filter_taps, cycle_counts, cycle_blocks).astype(jnp.bfloat16)
    banded = padded_2(fields, (("lat", 1),), 1, False)
    widened = padded_2(banded, (("lon", 2),), HALO, True)
    matrices = [
        banded_matrix(tap_table[0], lon_cols, 2 * HALO).reshape(3 * window_len, kernels * lon_cols)
    ]
    cycle_row = 0
    responses = [
        jnp.dot(
            widened.reshape(channels, 3 * window_len),
            matrices[cycle_row],
            preferred_element_type=jnp.float32,
        )
    ]
    response = (
        jnp.stack(responses, axis=1)
        .reshape(channels, lat_rows, kernels, lon_cols)
        .astype(jnp.bfloat16)
    )
    outputs = jnp.einsum(
        "koc,cikj->oij", weights, response, preferred_element_type=jnp.float32
    ).astype(jnp.bfloat16)
    response_grad = jnp.einsum(
        "koc,oij->cikj", weights, upstream, preferred_element_type=jnp.float32
    ).astype(jnp.bfloat16)
    grad_terms = jnp.einsum("oij,cikj->koc", upstream, response, preferred_element_type=jnp.float32)
    grad_share = lax.psum_scatter(grad_terms, "lon", scatter_dimension=1, tiled=True)
    weight_grad = lax.psum(grad_share, "lat")
    accumulated = jnp.zeros((channels, lat_rows + 2, window_len), jnp.float32)
    cycle_row = 0
    grad_piece = response_grad[:, cycle_row].reshape(channels, kernels * lon_cols)
    contrib = jnp.einsum(
        "cn,mn->cm", grad_piece, matrices[cycle_row], preferred_element_type=jnp.float32
    )
    accumulated = accumulated.at[:, cycle_row : cycle_row + 3].add(
        contrib.reshape(channels, 3, window_len)
    )
    rim_columns = jnp.concatenate(
        [accumulated[:, :, :HALO], accumulated[:, :, HALO + lon_cols :]], axis=2
    )
    arrived = padded_2(rim_columns, (("lon", 2),), HALO, True)
    interior = accumulated[:, :, HALO : HALO + lon_cols]
    interior = interior.at[:, :, :HALO].add(arrived[:, :, :HALO])
    interior = interior.at[:, :, lon_cols - HALO :].add(arrived[:, :, 3 * HALO :])
    edge_rows = jnp.stack([interior[:, 0], interior[:, lat_rows + 1]], axis=1)
    arrived = padded_2(edge_rows, (("lat", 1),), 1, False)
    result = interior[:, 1 : lat_rows + 1]
    result = result.at[:, 0].add(arrived[:, 0])
    result = result.at[:, lat_rows - 1].add(arrived[:, 3])
    return (outputs, result.astype(jnp.bfloat16), weight_grad)


def solution(mesh):
    return jax.shard_map(
        body,
        mesh=mesh,
        in_specs=(
            P("groups", "lat", "lon"),
            P("groups", "lat", "lon"),
            P(),
            P("lat", None, None, None, None),
            P("lat"),
            P("lat", None),
        ),
        out_specs=(P("groups", "lat", "lon"), P("groups", "lat", "lon"), P("groups", "lon", None)),
        check_vma=False,
    )
```

profile of v0, /device:TPU:0, one launch (start us, length us, event | category | flops | bytes accessed | tf_op | source)
XLA Modules:
  0.0 197.8 jit_solution(18379826614206599920)
XLA Ops:
  7.2 0.0 copy-start
  7.2 0.0 reduce-scatter.2.cloned.1.call-start
  7.2 1.0 copy.32
  8.3 1.3 collective-permute-start.1
  9.6 3.0 %collective-permute-start = (bf16[256,1,128]{0,2,1:T(8,128)(2,1)S(1)}, bf16[256,1,128]{0,2,1:T(8,128)(2,1)S(1)}, u32[]{:S(2)}, u32[]{:S(2)}) collective-permute-start(bf16[256,1,128]{0,2,1:T(8,128)(2,1)S(1)} %copy.32), channel_id=1, source_target_pairs={{0,4},{4,8},{8,12},{1,5},{5,9},{9,13},{2,6},{6,10},{10,14},{3,7},{... | collective-permute-start | bytes 196616 | tf_op jit(solution)/shard_map/ppermute | solution.py:17
  13.2 0.7 add_bitcast_fusion
  13.9 0.1 iota_add_fusion
  14.0 0.0 collective-permute-done
  14.0 5.1 %collective-permute-start.3 = (bf16[256,3,128]{0,2,1:T(8,128)(2,1)S(1)}, bf16[256,3,128]{0,2,1:T(8,128)(2,1)S(1)}, u32[]{:S(2)}, u32[]{:S(2)}) collective-permute-start(bf16[256,3,128]{0,2,1:T(8,128)(2,1)S(1)} %pad_maximum_fusion.1), channel_id=1, source_target_pairs={{1,0},{2,1},{3,2},{0,3},{5,4},{6,5},{7,6},{4,7},{9,8},{10,9},{11,1... | collective-permute-start | bytes 589832 | tf_op jit(solution)/shard_map/ppermute | solution.py:19
  19.1 0.9 fusion.3
  20.1 2.1 %tile.4 = bf16[9,3,128,385]{3,2,1,0:T(8,128)(2,1)} broadcast(bf16[9,3,385]{2,1,0:T(4,128)(2,1)S(1)} %concatenate.21.clone), dimensions={0,1,3} | broadcast | bytes 2681910 | tf_op jit(solution)/shard_map/tile | solution.py:47
  22.2 11.0 %tile.10 = bf16[9,3,49280]{2,1,0:T(4,128)(2,1)} reshape(bf16[9,3,128,385]{3,2,1,0:T(8,128)(2,1)} %tile.4) | data formatting | bytes 5322240 | tf_op jit(solution)/shard_map/tile | solution.py:47
  33.2 5.1 %slice.123 = bf16[9,3,49152]{2,1,0:T(4,128)(2,1)} slice(bf16[9,3,49280]{2,1,0:T(4,128)(2,1)} %tile.10), slice={[0:9], [0:3], [0:49152]} | slice | bytes 5308416 | tf_op jit(solution)/shard_map/slice | solution.py:47
  38.3 8.2 %reshape.267 = bf16[9,3,128,384]{3,2,1,0:T(8,128)(2,1)} reshape(bf16[9,3,49152]{2,1,0:T(4,128)(2,1)} %slice.123) | data formatting | bytes 5308416 | tf_op jit(solution)/shard_map/reshape | solution.py:48
  46.6 4.0 %copy.37 = bf16[3,384,9,128]{1,0,3,2:T(4,128)(2,1)S(1)} copy(bf16[3,384,9,128]{1,3,0,2:T(8,128)(2,1)} %bitcast.68) | data formatting | bytes 5308416 | tf_op jit(solution)/shard_map/transpose | solution.py:49
  50.6 0.5 copy.57
  51.1 0.0 collective-permute-done.3
  51.1 0.0 collective-permute-done.2
  51.2 0.0 copy-start.3
  51.2 1.1 convolution_convert_fusion.1
  52.3 0.0 copy-start.1
  52.3 0.8 copy-done.1
  53.1 0.5 convolution_bitcast_fusion
  53.6 3.4 %copy.44 = f32[9,256,256]{2,0,1:T(8,128)} copy(f32[9,256,256]{1,2,0:T(8,128)S(1)} %convolution_bitcast_fusion) | data formatting | bytes 4718592 | tf_op jit(solution)/shard_map/oij,cikj->koc/transpose | solution.py:81
  57.0 0.0 reduce-scatter.2.cloned.1.call-update
  57.0 0.0 copy-start.4
  57.0 0.0 all-reduce.3.cloned.1.call-start
  57.1 2.0 %copy.41 = bf16[3,384,9,128]{1,3,2,0:T(8,128)(2,1)S(1)} copy(bf16[3,384,9,128]{1,3,0,2:T(8,128)(2,1)} %bitcast.69) | data formatting | bytes 5308416 | tf_op jit(solution)/shard_map/transpose | solution.py:49
  59.1 0.3 convolution_convert_fusion
  59.5 1.0 fusion.22
  60.5 0.1 fusion.20
  60.6 0.1 collective-permute-start.4
  60.6 3.9 %collective-permute-start.5 = (f32[256,3,128]{2,0,1:T(8,128)S(1)}, f32[256,3,128]{2,0,1:T(8,128)S(1)}, u32[]{:S(2)}, u32[]{:S(2)}) collective-permute-start(f32[256,3,128]{2,0,1:T(8,128)S(1)} %get-tuple-element.97), channel_id=1, source_target_pairs={{1,0},{2,1},{3,2},{0,3},{5,4},{6,5},{7,6},{4,7},{9,8},{10,9},{11,1... | collective-permute-start | bytes 1179656 | tf_op jit(solution)/shard_map/ppermute | solution.py:19
  64.5 14.1 %collective-permute-done.4 = f32[256,3,128]{2,0,1:T(8,128)S(1)} collective-permute-done((f32[256,3,128]{2,0,1:T(8,128)S(1)}, f32[256,3,128]{2,0,1:T(8,128)S(1)}, u32[]{:S(2)}, u32[]{:S(2)}) %collective-permute-start.4) | collective-permute-done | bytes 393248 | tf_op jit(solution)/shard_map/ppermute | solution.py:17
  78.6 14.9 %collective-permute-done.5 = f32[256,3,128]{2,0,1:T(8,128)S(1)} collective-permute-done((f32[256,3,128]{2,0,1:T(8,128)S(1)}, f32[256,3,128]{2,0,1:T(8,128)S(1)}, u32[]{:S(2)}, u32[]{:S(2)}) %collective-permute-start.5) | collective-permute-done | bytes 393248 | tf_op jit(solution)/shard_map/ppermute | solution.py:19
  93.5 0.1 fusion.4
  93.6 0.0 copy-start.2
  93.6 1.5 collective-permute-start.6
  95.1 1.3 collective-permute-start.7
  96.4 53.4 %reduce-scatter.2.cloned.1.call-done = f32[9,64,256]{2,0,1:T(8,128)} async-done(((f32[9,256,256]{2,0,1:T(8,128)}), f32[9,64,256]{2,0,1:T(8,128)}) %reduce-scatter.2.cloned.1.call-update) | async-done | bytes 589840 | tf_op jit(solution)/shard_map/reduce_scatter | solution.py:82
  149.8 0.0 all-reduce.3.cloned.1.call-update
  149.8 0.5 fusion.1
  150.3 0.7 copy.45
  151.1 0.0 collective-permute-done.6
  151.1 0.0 collective-permute-done.7
  151.1 0.7 fusion.6
  151.7 36.9 %all-reduce.3.cloned.1.call-done = f32[9,64,256]{2,0,1:T(8,128)} async-done(((f32[9,64,256]{2,0,1:T(8,128)}), f32[9,64,256]{2,0,1:T(8,128)}) %all-reduce.3.cloned.1.call-update) | async-done | bytes 589840 | tf_op jit(solution)/shard_map/psum | solution.py:83
  188.6 2.4 %copy.46 = f32[9,64,256]{2,1,0:T(8,128)} copy(f32[9,64,256]{2,0,1:T(8,128)} %all-reduce.3.cloned.1.call-done) | data formatting | bytes 1179648
  (12 shorter events, 0.1 us)
Async XLA Ops:
  7.2 51.9 %copy-start = (bf16[9,256,256]{2,1,0:T(8,128)(2,1)S(1)}, bf16[9,256,256]{2,1,0:T(8,128)(2,1)}, u32[]{:S(2)}) copy-start(bf16[9,256,256]{2,1,0:T(8,128)(2,1)} %param.24) | copy-start | bytes 3538948
  7.2 142.6 %reduce-scatter.2.cloned.1.call-start = ((), (), s32[]{:S(2)}) async-start(), calls=%async_computation.1 | async-start | bytes 5242880 | tf_op jit(solution)/shard_map/reduce_scatter | solution.py:82
  8.3 5.7 %collective-permute-start.1 = (bf16[256,1,128]{0,2,1:T(8,128)(2,1)S(1)}, bf16[256,1,128]{0,2,1:T(8,128)(2,1)S(1)}, u32[]{:S(2)}, u32[]{:S(2)}) collective-permute-start(bf16[256,1,128]{0,2,1:T(8,128)(2,1)S(1)} %copy.32), channel_id=1, source_target_pairs={{4,0},{8,4},{12,8},{5,1},{9,5},{13,9},{6,2},{10,6},{14,10},{7,3},{... | collective-permute-start | bytes 196616 | tf_op jit(solution)/shard_map/ppermute | solution.py:19
  9.6 4.4 %collective-permute-start = (bf16[256,1,128]{0,2,1:T(8,128)(2,1)S(1)}, bf16[256,1,128]{0,2,1:T(8,128)(2,1)S(1)}, u32[]{:S(2)}, u32[]{:S(2)}) collective-permute-start(bf16[256,1,128]{0,2,1:T(8,128)(2,1)S(1)} %copy.32), channel_id=1, source_target_pairs={{0,4},{4,8},{8,12},{1,5},{5,9},{9,13},{2,6},{6,10},{10,14},{3,7},{... | collective-permute-start | bytes 196616 | tf_op jit(solution)/shard_map/ppermute | solution.py:17
  14.0 37.1 %collective-permute-start.3 = (bf16[256,3,128]{0,2,1:T(8,128)(2,1)S(1)}, bf16[256,3,128]{0,2,1:T(8,128)(2,1)S(1)}, u32[]{:S(2)}, u32[]{:S(2)}) collective-permute-start(bf16[256,3,128]{0,2,1:T(8,128)(2,1)S(1)} %pad_maximum_fusion.1), channel_id=1, source_target_pairs={{1,0},{2,1},{3,2},{0,3},{5,4},{6,5},{7,6},{4,7},{9,8},{10,9},{11,1... | collective-permute-start | bytes 589832 | tf_op jit(solution)/shard_map/ppermute | solution.py:19
  19.1 32.0 %collective-permute-start.2 = (bf16[256,3,128]{0,2,1:T(8,128)(2,1)S(1)}, bf16[256,3,128]{0,2,1:T(8,128)(2,1)S(1)}, u32[]{:S(2)}, u32[]{:S(2)}) collective-permute-start(bf16[256,3,128]{0,2,1:T(8,128)(2,1)S(1)} %pad_maximum_fusion.1), channel_id=1, source_target_pairs={{0,1},{1,2},{2,3},{3,0},{4,5},{5,6},{6,7},{7,4},{8,9},{9,10},{10,1... | collective-permute-start | bytes 589832 | tf_op jit(solution)/shard_map/ppermute | solution.py:17
  51.2 1.9 copy-start.3
  52.3 0.8 copy-start.1
  57.0 2.1 %copy-start.4 = (bf16[256,1,128]{2,0,1:T(8,128)(2,1)S(1)}, bf16[256,1,128]{2,0,1:T(8,128)(2,1)}, u32[]{:S(2)}) copy-start(bf16[256,1,128]{2,0,1:T(8,128)(2,1)} %param.23) | copy-start | bytes 196612
  57.0 131.6 %all-reduce.3.cloned.1.call-start = ((), (), s32[]{:S(2)}) async-start(), calls=%async_computation.2 | async-start | bytes 2097152 | tf_op jit(solution)/shard_map/psum | solution.py:83
  60.6 18.0 %collective-permute-start.4 = (f32[256,3,128]{2,0,1:T(8,128)S(1)}, f32[256,3,128]{2,0,1:T(8,128)S(1)}, u32[]{:S(2)}, u32[]{:S(2)}) collective-permute-start(f32[256,3,128]{2,0,1:T(8,128)S(1)} %get-tuple-element.96), channel_id=1, source_target_pairs={{0,1},{1,2},{2,3},{3,0},{4,5},{5,6},{6,7},{7,4},{8,9},{9,10},{10,1... | collective-permute-start | bytes 1179656 | tf_op jit(solution)/shard_map/ppermute | solution.py:17
  60.6 32.9 %collective-permute-start.5 = (f32[256,3,128]{2,0,1:T(8,128)S(1)}, f32[256,3,128]{2,0,1:T(8,128)S(1)}, u32[]{:S(2)}, u32[]{:S(2)}) collective-permute-start(f32[256,3,128]{2,0,1:T(8,128)S(1)} %get-tuple-element.97), channel_id=1, source_target_pairs={{1,0},{2,1},{3,2},{0,3},{5,4},{6,5},{7,6},{4,7},{9,8},{10,9},{11,1... | collective-permute-start | bytes 1179656 | tf_op jit(solution)/shard_map/ppermute | solution.py:19
  93.6 56.2 %copy-start.2 = (bf16[256,9,128]{2,0,1:T(8,128)(2,1)S(1)}, bf16[256,9,128]{2,0,1:T(8,128)(2,1)}, u32[]{:S(2)}) copy-start(bf16[256,9,128]{2,0,1:T(8,128)(2,1)} %copy-done.1) | copy-start | bytes 1769476
  93.6 57.5 %collective-permute-start.6 = (f32[256,1,128]{2,0,1:T(8,128)S(1)}, f32[256,1,128]{2,0,1:T(8,128)S(1)}, u32[]{:S(2)}, u32[]{:S(2)}) collective-permute-start(f32[256,1,128]{2,0,1:T(8,128)S(1)} %get-tuple-element.98), channel_id=1, source_target_pairs={{0,4},{4,8},{8,12},{1,5},{5,9},{9,13},{2,6},{6,10},{10,14},{3,7},{... | collective-permute-start | bytes 393224 | tf_op jit(solution)/shard_map/ppermute | solution.py:17
  95.1 56.0 %collective-permute-start.7 = (f32[256,1,128]{2,0,1:T(8,128)S(1)}, f32[256,1,128]{2,0,1:T(8,128)S(1)}, u32[]{:S(2)}, u32[]{:S(2)}) collective-permute-start(f32[256,1,128]{2,0,1:T(8,128)S(1)} %get-tuple-element.99), channel_id=1, source_target_pairs={{4,0},{8,4},{12,8},{5,1},{9,5},{13,9},{6,2},{10,6},{14,10},{7,3},{... | collective-permute-start | bytes 393224 | tf_op jit(solution)/shard_map/ppermute | solution.py:19
Sparse Core Ops, SparseCore 0:
  57.1 92.6 reduce-scatter.1
  152.2 36.3 all-reduce.2
where the time goes:
time: 199 us; the launch traced here: 198 us
  waiting for transfers between devices  119 us (60%)
  local copies, waits for them, and re-layouts  41.5 us (21%)
  starting transfers between devices  16.2 us (8%)
  between operations  14.9 us (7%)
  matrix products  4.39 us (2%)
    reduce_scatter x1, waiting for transfers between devices, body(): lax.psum_scatter(grad_terms, 'lon', scatter_dimension=1, tiled=True)  53.4 us
    psum x1, waiting for transfers between devices, body(): weight_grad = lax.psum(grad_share, 'lat')  36.9 us
    ppermute x4, waiting for transfers between devices, padded_2(): lax.ppermute(head, axis, [((i + 1) % count, i) for i in range(ends)])  14.9 us
    ppermute x4, waiting for transfers between devices, padded_2(): lax.ppermute(tail, axis, [(i, (i + 1) % count) for i in range(ends)])  14.1 us
    another operation x2, local copies, waits for them, and re-layouts, banded_matrix(): jnp.tile(padded, (1, 1, out_width))[:, :, :out_width * window_len]  13.1 us
    ppermute x4, starting transfers between devices, padded_2(): lax.ppermute(head, axis, [((i + 1) % count, i) for i in range(ends)])  11.6 us
    reshape x1, local copies, waits for them, and re-layouts, banded_matrix(): repeated = repeated.reshape(kernels, stencil_rows, out_width, window_len)  8.24 us
    transpose x2, local copies, waits for them, and re-layouts, banded_matrix(): return jnp.transpose(repeated, (1, 3, 0, 2))  6.08 us
  transfers between devices with their start and end apart: 10, of which 4 were waited for; matrix products, arithmetic and copies ran while one was open for 19% of the time, Pallas kernels for 0%

commit v1 on v0

--- a/solution.py
+++ b/solution.py
@@ -80,7 +80,7 @@
     ).astype(jnp.bfloat16)
     grad_terms = jnp.einsum("oij,cikj->koc", upstream, response, preferred_element_type=jnp.float32)
     grad_share = lax.psum_scatter(grad_terms, "lon", scatter_dimension=1, tiled=True)
-    weight_grad = lax.psum(grad_share, "lat")
+    weight_grad = jnp.sum(lax.all_gather(grad_share, "lat"), axis=0)
     accumulated = jnp.zeros((channels, lat_rows + 2, window_len), jnp.float32)
     cycle_row = 0
     grad_piece = response_grad[:, cycle_row].reshape(channels, kernels * lon_cols)

time: 199 us -> 185 us (0.930)
  the two profiles are of different devices: /device:TPU:0 before, /device:TPU:1 now
where the time goes in v1:
time: 185 us; the launch traced here: 184 us
  waiting for transfers between devices  99.6 us (54%)
  local copies, waits for them, and re-layouts  41.6 us (22%)
  starting transfers between devices  18.9 us (10%)
  between operations  14.9 us (8%)
  matrix products  4.4 us (2%)
  other arithmetic  4.24 us (2%)
    reduce_scatter x1, waiting for transfers between devices, body(): lax.psum_scatter(grad_terms, 'lon', scatter_dimension=1, tiled=True)  79.1 us
    another operation x2, local copies, waits for them, and re-layouts, banded_matrix(): jnp.tile(padded, (1, 1, out_width))[:, :, :out_width * window_len]  13.1 us
    ppermute x4, waiting for transfers between devices, padded_2(): lax.ppermute(head, axis, [((i + 1) % count, i) for i in range(ends)])  11.9 us
    ppermute x4, starting transfers between devices, padded_2(): lax.ppermute(tail, axis, [(i, (i + 1) % count) for i in range(ends)])  9.54 us
    ppermute x4, starting transfers between devices, padded_2(): lax.ppermute(head, axis, [((i + 1) % count, i) for i in range(ends)])  9.29 us
    ppermute x4, waiting for transfers between devices, padded_2(): lax.ppermute(tail, axis, [(i, (i + 1) % count) for i in range(ends)])  8.61 us
    reshape x1, local copies, waits for them, and re-layouts, banded_matrix(): repeated = repeated.reshape(kernels, stencil_rows, out_width, window_len)  8.24 us
    transpose x2, local copies, waits for them, and re-layouts, banded_matrix(): return jnp.transpose(repeated, (1, 3, 0, 2))  6.11 us
  transfers between devices with their start and end apart: 10, of which 4 were waited for; matrix products, arithmetic and copies ran while one was open for 21% of the time, Pallas kernels for 0%

profile of v1, /device:TPU:1, one launch (start us, length us, event | category | flops | bytes accessed | tf_op | source)
XLA Modules:
  0.0 183.7 jit_solution(18091772679872770563)
XLA Ops:
  7.2 0.0 copy-start
  7.2 0.0 reduce-scatter.2.cloned.1.call-start
  7.2 1.0 copy.30
  8.3 2.0 %collective-permute-start.1 = (bf16[256,1,128]{0,2,1:T(8,128)(2,1)S(1)}, bf16[256,1,128]{0,2,1:T(8,128)(2,1)S(1)}, u32[]{:S(2)}, u32[]{:S(2)}) collective-permute-start(bf16[256,1,128]{0,2,1:T(8,128)(2,1)S(1)} %copy.30), channel_id=1, source_target_pairs={{4,0},{8,4},{12,8},{5,1},{9,5},{13,9},{6,2},{10,6},{14,10},{7,3},{... | collective-permute-start | bytes 196616 | tf_op jit(solution)/shard_map/ppermute | solution.py:19
  10.2 4.5 %collective-permute-start = (bf16[256,1,128]{0,2,1:T(8,128)(2,1)S(1)}, bf16[256,1,128]{0,2,1:T(8,128)(2,1)S(1)}, u32[]{:S(2)}, u32[]{:S(2)}) collective-permute-start(bf16[256,1,128]{0,2,1:T(8,128)(2,1)S(1)} %copy.30), channel_id=1, source_target_pairs={{0,4},{4,8},{8,12},{1,5},{5,9},{9,13},{2,6},{6,10},{10,14},{3,7},{... | collective-permute-start | bytes 196616 | tf_op jit(solution)/shard_map/ppermute | solution.py:17
  15.3 0.7 add_bitcast_fusion
  16.0 0.1 iota_add_fusion
  16.1 0.0 collective-permute-done.1
  16.1 0.0 collective-permute-done
  16.1 3.4 %collective-permute-start.3 = (bf16[256,3,128]{0,2,1:T(8,128)(2,1)S(1)}, bf16[256,3,128]{0,2,1:T(8,128)(2,1)S(1)}, u32[]{:S(2)}, u32[]{:S(2)}) collective-permute-start(bf16[256,3,128]{0,2,1:T(8,128)(2,1)S(1)} %pad_maximum_fusion.1), channel_id=1, source_target_pairs={{1,0},{2,1},{3,2},{0,3},{5,4},{6,5},{7,6},{4,7},{9,8},{10,9},{11,1... | collective-permute-start | bytes 589832 | tf_op jit(solution)/shard_map/ppermute | solution.py:19
  19.5 0.0 collective-permute-start.2
  19.5 0.9 fusion.3
  20.5 2.1 %tile.4 = bf16[9,3,128,385]{3,2,1,0:T(8,128)(2,1)} broadcast(bf16[9,3,385]{2,1,0:T(4,128)(2,1)S(1)} %concatenate.21.clone), dimensions={0,1,3} | broadcast | bytes 2681910 | tf_op jit(solution)/shard_map/tile | solution.py:47
  22.5 11.0 %tile.10 = bf16[9,3,49280]{2,1,0:T(4,128)(2,1)} reshape(bf16[9,3,128,385]{3,2,1,0:T(8,128)(2,1)} %tile.4) | data formatting | bytes 5322240 | tf_op jit(solution)/shard_map/tile | solution.py:47
  33.6 5.1 %slice.123 = bf16[9,3,49152]{2,1,0:T(4,128)(2,1)} slice(bf16[9,3,49280]{2,1,0:T(4,128)(2,1)} %tile.10), slice={[0:9], [0:3], [0:49152]} | slice | bytes 5308416 | tf_op jit(solution)/shard_map/slice | solution.py:47
  38.7 8.2 %reshape.267 = bf16[9,3,128,384]{3,2,1,0:T(8,128)(2,1)} reshape(bf16[9,3,49152]{2,1,0:T(4,128)(2,1)} %slice.123) | data formatting | bytes 5308416 | tf_op jit(solution)/shard_map/reshape | solution.py:48
  46.9 4.0 %copy.35 = bf16[3,384,9,128]{1,0,3,2:T(4,128)(2,1)S(1)} copy(bf16[3,384,9,128]{1,3,0,2:T(8,128)(2,1)} %bitcast.69) | data formatting | bytes 5308416 | tf_op jit(solution)/shard_map/transpose | solution.py:49
  51.0 0.5 copy.58
  51.5 0.0 collective-permute-done.3
  51.5 0.0 copy-start.3
  51.5 1.1 convolution_convert_fusion.1
  52.6 0.0 copy-start.1
  52.7 0.8 copy-done.1
  53.5 0.5 convolution_bitcast_fusion
  53.9 3.4 %copy.42 = f32[9,256,256]{2,0,1:T(8,128)} copy(f32[9,256,256]{1,2,0:T(8,128)S(1)} %convolution_bitcast_fusion) | data formatting | bytes 4718592 | tf_op jit(solution)/shard_map/oij,cikj->koc/transpose | solution.py:81
  57.4 0.0 reduce-scatter.2.cloned.1.call-update
  57.4 0.0 all-gather.3.cloned.1.call-start
  57.4 79.1 %reduce-scatter.2.cloned.1.call-done = f32[9,64,256]{2,0,1:T(8,128)} async-done(((f32[9,256,256]{2,0,1:T(8,128)}), f32[9,64,256]{2,0,1:T(8,128)}) %reduce-scatter.2.cloned.1.call-update) | async-done | bytes 589840 | tf_op jit(solution)/shard_map/reduce_scatter | solution.py:82
  136.6 2.4 %copy.43 = f32[9,64,256]{2,1,0:T(8,128)} copy(f32[9,64,256]{2,0,1:T(8,128)} %reduce-scatter.2.cloned.1.call-done) | data formatting | bytes 1179648 | tf_op jit(solution)/shard_map/reduce_scatter | solution.py:82
  139.0 0.0 all-gather.3.cloned.1.call-update
  139.0 0.0 copy-start.4
  139.0 2.1 %copy.39 = bf16[3,384,9,128]{1,3,2,0:T(8,128)(2,1)S(1)} copy(bf16[3,384,9,128]{1,3,0,2:T(8,128)(2,1)} %bitcast.70) | data formatting | bytes 5308416 | tf_op jit(solution)/shard_map/transpose | solution.py:49
  141.1 0.3 convolution_convert_fusion
  141.5 1.0 fusion.22
  142.5 0.1 fusion.20
  142.6 0.0 copy-start.2
  142.6 1.3 collective-permute-start.4
  143.9 2.0 %collective-permute-start.5 = (f32[256,3,128]{2,0,1:T(8,128)S(1)}, f32[256,3,128]{2,0,1:T(8,128)S(1)}, u32[]{:S(2)}, u32[]{:S(2)}) collective-permute-start(f32[256,3,128]{2,0,1:T(8,128)S(1)} %get-tuple-element.97), channel_id=1, source_target_pairs={{1,0},{2,1},{3,2},{0,3},{5,4},{6,5},{7,6},{4,7},{9,8},{10,9},{11,1... | collective-permute-start | bytes 1179656 | tf_op jit(solution)/shard_map/ppermute | solution.py:19
  145.9 8.6 %collective-permute-done.4 = f32[256,3,128]{2,0,1:T(8,128)S(1)} collective-permute-done((f32[256,3,128]{2,0,1:T(8,128)S(1)}, f32[256,3,128]{2,0,1:T(8,128)S(1)}, u32[]{:S(2)}, u32[]{:S(2)}) %collective-permute-start.4) | collective-permute-done | bytes 393248 | tf_op jit(solution)/shard_map/ppermute | solution.py:17
  154.5 8.8 %collective-permute-done.5 = f32[256,3,128]{2,0,1:T(8,128)S(1)} collective-permute-done((f32[256,3,128]{2,0,1:T(8,128)S(1)}, f32[256,3,128]{2,0,1:T(8,128)S(1)}, u32[]{:S(2)}, u32[]{:S(2)}) %collective-permute-start.5) | collective-permute-done | bytes 393248 | tf_op jit(solution)/shard_map/ppermute | solution.py:19
  163.3 0.1 fusion.4
  163.4 3.8 %collective-permute-start.6 = (f32[256,1,128]{2,0,1:T(8,128)S(1)}, f32[256,1,128]{2,0,1:T(8,128)S(1)}, u32[]{:S(2)}, u32[]{:S(2)}) collective-permute-start(f32[256,1,128]{2,0,1:T(8,128)S(1)} %get-tuple-element.98), channel_id=1, source_target_pairs={{0,4},{4,8},{8,12},{1,5},{5,9},{9,13},{2,6},{6,10},{10,14},{3,7},{... | collective-permute-start | bytes 393224 | tf_op jit(solution)/shard_map/ppermute | solution.py:17
  167.2 1.9 %collective-permute-start.7 = (f32[256,1,128]{2,0,1:T(8,128)S(1)}, f32[256,1,128]{2,0,1:T(8,128)S(1)}, u32[]{:S(2)}, u32[]{:S(2)}) collective-permute-start(f32[256,1,128]{2,0,1:T(8,128)S(1)} %get-tuple-element.99), channel_id=1, source_target_pairs={{4,0},{8,4},{12,8},{5,1},{9,5},{13,9},{6,2},{10,6},{14,10},{7,3},{... | collective-permute-start | bytes 393224 | tf_op jit(solution)/shard_map/ppermute | solution.py:19
  169.1 0.6 fusion.1
  169.7 0.7 copy.45
  170.4 3.1 %collective-permute-done.7 = f32[256,1,128]{2,0,1:T(8,128)S(1)} collective-permute-done((f32[256,1,128]{2,0,1:T(8,128)S(1)}, f32[256,1,128]{2,0,1:T(8,128)S(1)}, u32[]{:S(2)}, u32[]{:S(2)}) %collective-permute-start.7) | collective-permute-done | bytes 131104 | tf_op jit(solution)/shard_map/ppermute | solution.py:19
  173.5 0.7 fusion.6
  174.1 2.7 %reduce_sum.9 = f32[9,64,256]{2,1,0:T(8,128)} reduce(f32[4,9,64,256]{3,2,1,0:T(8,128)} %bitcast.74, f32[]{:T(128)} %constant.148.clone.1), dimensions={0}, to_apply=%region_1.2 | reduce | flops 442368 | bytes 2949124 | tf_op jit(solution)/shard_map/reduce_sum | solution.py:83
  (13 shorter events, 0.1 us)
Async XLA Ops:
  7.2 133.9 %copy-start = (bf16[9,256,256]{2,1,0:T(8,128)(2,1)S(1)}, bf16[9,256,256]{2,1,0:T(8,128)(2,1)}, u32[]{:S(2)}) copy-start(bf16[9,256,256]{2,1,0:T(8,128)(2,1)} %param.24) | copy-start | bytes 3538948
  7.2 129.4 %reduce-scatter.2.cloned.1.call-start = ((), (), s32[]{:S(2)}) async-start(), calls=%async_computation.1 | async-start | bytes 5242880 | tf_op jit(solution)/shard_map/reduce_scatter | solution.py:82
  8.3 7.8 %collective-permute-start.1 = (bf16[256,1,128]{0,2,1:T(8,128)(2,1)S(1)}, bf16[256,1,128]{0,2,1:T(8,128)(2,1)S(1)}, u32[]{:S(2)}, u32[]{:S(2)}) collective-permute-start(bf16[256,1,128]{0,2,1:T(8,128)(2,1)S(1)} %copy.30), channel_id=1, source_target_pairs={{4,0},{8,4},{12,8},{5,1},{9,5},{13,9},{6,2},{10,6},{14,10},{7,3},{... | collective-permute-start | bytes 196616 | tf_op jit(solution)/shard_map/ppermute | solution.py:19
  10.2 5.9 %collective-permute-start = (bf16[256,1,128]{0,2,1:T(8,128)(2,1)S(1)}, bf16[256,1,128]{0,2,1:T(8,128)(2,1)S(1)}, u32[]{:S(2)}, u32[]{:S(2)}) collective-permute-start(bf16[256,1,128]{0,2,1:T(8,128)(2,1)S(1)} %copy.30), channel_id=1, source_target_pairs={{0,4},{4,8},{8,12},{1,5},{5,9},{9,13},{2,6},{6,10},{10,14},{3,7},{... | collective-permute-start | bytes 196616 | tf_op jit(solution)/shard_map/ppermute | solution.py:17
  16.1 35.3 %collective-permute-start.3 = (bf16[256,3,128]{0,2,1:T(8,128)(2,1)S(1)}, bf16[256,3,128]{0,2,1:T(8,128)(2,1)S(1)}, u32[]{:S(2)}, u32[]{:S(2)}) collective-permute-start(bf16[256,3,128]{0,2,1:T(8,128)(2,1)S(1)} %pad_maximum_fusion.1), channel_id=1, source_target_pairs={{1,0},{2,1},{3,2},{0,3},{5,4},{6,5},{7,6},{4,7},{9,8},{10,9},{11,1... | collective-permute-start | bytes 589832 | tf_op jit(solution)/shard_map/ppermute | solution.py:19
  19.5 32.0 %collective-permute-start.2 = (bf16[256,3,128]{0,2,1:T(8,128)(2,1)S(1)}, bf16[256,3,128]{0,2,1:T(8,128)(2,1)S(1)}, u32[]{:S(2)}, u32[]{:S(2)}) collective-permute-start(bf16[256,3,128]{0,2,1:T(8,128)(2,1)S(1)} %pad_maximum_fusion.1), channel_id=1, source_target_pairs={{0,1},{1,2},{2,3},{3,0},{4,5},{5,6},{6,7},{7,4},{8,9},{9,10},{10,1... | collective-permute-start | bytes 589832 | tf_op jit(solution)/shard_map/ppermute | solution.py:17
  51.5 1.9 %copy-start.3 = (bf16[256,1,128]{2,0,1:T(8,128)(2,1)S(1)}, bf16[256,1,128]{2,0,1:T(8,128)(2,1)}, u32[]{:S(2)}) copy-start(bf16[256,1,128]{2,0,1:T(8,128)(2,1)} %param.23) | copy-start | bytes 196612
  52.6 0.8 copy-start.1
  57.4 116.7 %all-gather.3.cloned.1.call-start = ((), (), s32[]{:S(2)}) async-start(), calls=%async_computation.2 | async-start | bytes 2949120 | tf_op jit(solution)/shard_map/all_gather | solution.py:83
  139.0 2.1 %copy-start.4 = (bf16[256,1,128]{2,0,1:T(8,128)(2,1)S(1)}, bf16[256,1,128]{2,0,1:T(8,128)(2,1)}, u32[]{:S(2)}) copy-start(bf16[256,1,128]{2,0,1:T(8,128)(2,1)} %param.23) | copy-start | bytes 196612
  142.6 26.6 %copy-start.2 = (bf16[256,9,128]{2,0,1:T(8,128)(2,1)S(1)}, bf16[256,9,128]{2,0,1:T(8,128)(2,1)}, u32[]{:S(2)}) copy-start(bf16[256,9,128]{2,0,1:T(8,128)(2,1)} %copy-done.1) | copy-start | bytes 1769476
  142.6 11.9 %collective-permute-start.4 = (f32[256,3,128]{2,0,1:T(8,128)S(1)}, f32[256,3,128]{2,0,1:T(8,128)S(1)}, u32[]{:S(2)}, u32[]{:S(2)}) collective-permute-start(f32[256,3,128]{2,0,1:T(8,128)S(1)} %get-tuple-element.96), channel_id=1, source_target_pairs={{0,1},{1,2},{2,3},{3,0},{4,5},{5,6},{6,7},{7,4},{8,9},{9,10},{10,1... | collective-permute-start | bytes 1179656 | tf_op jit(solution)/shard_map/ppermute | solution.py:17
  143.9 19.4 %collective-permute-start.5 = (f32[256,3,128]{2,0,1:T(8,128)S(1)}, f32[256,3,128]{2,0,1:T(8,128)S(1)}, u32[]{:S(2)}, u32[]{:S(2)}) collective-permute-start(f32[256,3,128]{2,0,1:T(8,128)S(1)} %get-tuple-element.97), channel_id=1, source_target_pairs={{1,0},{2,1},{3,2},{0,3},{5,4},{6,5},{7,6},{4,7},{9,8},{10,9},{11,1... | collective-permute-start | bytes 1179656 | tf_op jit(solution)/shard_map/ppermute | solution.py:19
  163.4 7.0 %collective-permute-start.6 = (f32[256,1,128]{2,0,1:T(8,128)S(1)}, f32[256,1,128]{2,0,1:T(8,128)S(1)}, u32[]{:S(2)}, u32[]{:S(2)}) collective-permute-start(f32[256,1,128]{2,0,1:T(8,128)S(1)} %get-tuple-element.98), channel_id=1, source_target_pairs={{0,4},{4,8},{8,12},{1,5},{5,9},{9,13},{2,6},{6,10},{10,14},{3,7},{... | collective-permute-start | bytes 393224 | tf_op jit(solution)/shard_map/ppermute | solution.py:17
  167.2 6.3 %collective-permute-start.7 = (f32[256,1,128]{2,0,1:T(8,128)S(1)}, f32[256,1,128]{2,0,1:T(8,128)S(1)}, u32[]{:S(2)}, u32[]{:S(2)}) collective-permute-start(f32[256,1,128]{2,0,1:T(8,128)S(1)} %get-tuple-element.99), channel_id=1, source_target_pairs={{4,0},{8,4},{12,8},{5,1},{9,5},{13,9},{6,2},{10,6},{14,10},{7,3},{... | collective-permute-start | bytes 393224 | tf_op jit(solution)/shard_map/ppermute | solution.py:19
Sparse Core Ops, SparseCore 0:
  57.5 79.0 reduce-scatter.1
  139.1 24.9 all-gather.2
